TPU v7x, 256 devices: a whole 4x4x8 slice. The times are simulated.
256 devices in a mesh: seq: 8 (over z), exp: 8 (over x, y_hi), img: 4 (over y_lo, core).
Axes of the slice: x: 4, y: 4 (y_hi: 2, y_lo: 2; y = y_hi * 2 + y_lo), z: 8, core: 2. Of those that a mesh axis runs over, the one named last changes fastest.
Arguments:
- projected: bfloat16 [32, 1024, 3, 1280], P(('img', 'exp'), 'seq'), parts along dimension 0, may hold values from -6 to 6
- residual: bfloat16 [32, 1024, 1280], P(('img', 'exp'), 'seq'), parts along dimension 0, may hold values from -6 to 6
- attn_proj: bfloat16 [1280, 1280], P('seq'), may hold values from -0.15625 to 0.15625
- norm_gain: float32 [1280], replicated, may hold values from 0.5 to 2
- norm_bias: float32 [1280], replicated, may hold values from -3 to 3
- expert_ids: int32 [32, 1024, 1], P(('img', 'exp')), parts along dimension 0, may hold values from 0 to 15; in each aligned block of 128 rows (0 to 127, 128 to 255, ..., all dimensions but the last counted through in order) at most 12 rows name the same one
- expert_up: bfloat16 [16, 1280, 5120], P('exp', None, 'seq'), may hold values from -0.15625 to 0.15625
- expert_down: bfloat16 [16, 5120, 1280], P('exp', 'seq'), may hold values from -0.078125 to 0.078125
Outputs:
- layer_out: bfloat16 [32, 1024, 1280], P(('img', 'exp'), 'seq'), parts along dimension 0
There are 4 independent parts, one for each index of `img`. A program takes and returns all parts, laid end to end along the dimension named above; an argument that names none is the same for every part. Nothing has to cross between parts.
Inputs may be any that keep to these rules, and one draw needn't show every extreme that they name: `expert_ids`: in each sequence, within every aligned block of 128 tokens, no expert is named by more than 12 tokens.
All inputs are finite; a program needn't handle non-finite values.
Results may differ from a plain program's by a relative error of at most 0.015.
Values may be sent and summed in bfloat16 or wider, within the bound.
No kernel may reach another device: no remote copies, remote signals or barrier semaphores. Data moves between devices by JAX's collectives and lax.ppermute only.
A program may use at most 64 MiB of HBM per device.

v0:
```python
import jax
import jax.numpy as jnp
from jax import lax
from jax.sharding import PartitionSpec as P

HEADS = 16
HEAD_DIM = 80


def attend(gathered):
    queries = gathered[:, 0, 0]
    keys_all = gathered[:, 1, 0]
    values = gathered[:, 2, 0]
    length = queries.shape[0]
    span_rows = min(512, length)
    factor = 1.0 / queries.shape[2] ** 0.5

    def one_block(offset):
        query_rows = lax.dynamic_slice_in_dim(queries, offset, span_rows, 0)
        scores = (
            jnp.einsum("qhd,khd->hqk", query_rows, keys_all, preferred_element_type=jnp.float32)
            * factor
        )
        peak = jnp.max(scores, axis=-1, keepdims=True)
        powers = jnp.exp(scores - peak)
        weights = (powers / jnp.sum(powers, axis=-1, keepdims=True)).astype(jnp.bfloat16)
        mixed = jnp.einsum("hqk,khd->qhd", weights, values, preferred_element_type=jnp.float32)
        return mixed.astype(jnp.bfloat16)

    starts = jnp.arange(length // span_rows, dtype=jnp.int32) * span_rows
    blocks = lax.map(one_block, starts)
    return blocks.reshape(length, queries.shape[1], queries.shape[2])


def layer_norm(stream, norm_gain, norm_bias):
    values = stream.astype(jnp.float32)
    centre = jnp.mean(values, axis=-1, keepdims=True)
    centered = values - centre
    variance = jnp.mean(centered * centered, axis=-1, keepdims=True)
    return (centered / jnp.sqrt(variance + 1e-06) * norm_gain + norm_bias).astype(jnp.bfloat16)


def per_device(
    projected, residual, attn_proj, norm_gain, norm_bias, expert_ids, expert_up, expert_down
):
    tok_rows = projected.shape[1]
    model_width = projected.shape[3]
    seq_count = lax.axis_size("seq")
    exp_count = lax.axis_size("exp")
    local_experts = expert_up.shape[0]
    experts = local_experts * exp_count
    cap_dev = 3 * tok_rows // (2 * experts)
    capacity = cap_dev * seq_count
    length = tok_rows * seq_count
    heads_here = HEADS // seq_count
    head_width = heads_here * HEAD_DIM
    regrouped = projected[0].reshape(tok_rows, 3, seq_count, heads_here, HEAD_DIM)
    attended = attend(lax.all_to_all(regrouped, "seq", split_axis=2, concat_axis=0, tiled=True))
    attended = attended.reshape(seq_count, tok_rows, 1, head_width)
    token_heads = lax.all_to_all(attended, "seq", split_axis=0, concat_axis=2, tiled=True).reshape(
        tok_rows, model_width
    )
    projected_sum = jnp.dot(
        token_heads,
        lax.all_gather(attn_proj, "seq", axis=0, tiled=True),
        preferred_element_type=jnp.float32,
    )
    stream_own = residual[0].astype(jnp.float32) + projected_sum
    stream = stream_own.astype(jnp.bfloat16)
    stream_own = stream.astype(jnp.float32)
    normed = layer_norm(stream, norm_gain, norm_bias)
    ids_flat = expert_ids[0, :, 0]
    onehot = (ids_flat[:, None] == jnp.arange(experts, dtype=jnp.int32)[None, :]).astype(jnp.int32)
    blocks = onehot.reshape(seq_count, tok_rows, experts)
    before = jnp.cumsum(blocks, axis=1) - blocks
    order_in_block = jnp.sum(before * blocks, axis=2).reshape(length)
    block_id = jnp.arange(length, dtype=jnp.int32) // tok_rows
    slot_all = ids_flat * capacity + block_id * cap_dev + order_in_block
    normed_all = lax.all_gather(normed, "seq", axis=0, tiled=True)
    buffer = jnp.zeros((experts * capacity, model_width), jnp.bfloat16).at[slot_all].set(normed_all)
    buffer = buffer.reshape(exp_count, local_experts, capacity, model_width)
    arrived = lax.all_to_all(buffer, "exp", split_axis=0, concat_axis=0, tiled=True)
    hidden = jax.nn.gelu(
        jnp.einsum("secd,edf->secf", arrived, expert_up, preferred_element_type=jnp.float32),
        approximate=False,
    ).astype(jnp.bfloat16)
    pieces = jnp.einsum(
        "secf,efd->secd", hidden, expert_down, preferred_element_type=jnp.float32
    ).astype(jnp.bfloat16)
    returned = lax.all_to_all(pieces, "exp", split_axis=0, concat_axis=0, tiled=True).reshape(
        experts * capacity, model_width
    )
    per_token = jnp.take(returned, slot_all, axis=0).astype(jnp.float32)
    expert_out = lax.psum_scatter(
        per_token.astype(jnp.bfloat16), "seq", scatter_dimension=0, tiled=True
    ).astype(jnp.float32)
    return (stream_own + expert_out).astype(jnp.bfloat16)[None]


def solution(mesh):
    return jax.shard_map(
        per_device,
        mesh=mesh,
        in_specs=(
            P(("img", "exp"), "seq", None, None),
            P(("img", "exp"), "seq", None),
            P("seq", None),
            P(),
            P(),
            P(("img", "exp"), None, None),
            P("exp", None, "seq"),
            P("exp", "seq", None),
        ),
        out_specs=P(("img", "exp"), "seq", None),
        check_vma=False,
    )
```

profile of v0, /device:TPU:8, one launch (start us, length us, event | category | flops | bytes accessed | tf_op | source)
XLA Modules:
  0.0 343.8 jit_solution(7028651593634963282)
XLA Ops:
  6.5 0.0 copy-start
  6.5 0.0 all-gather.3.cloned.1.call-start
  6.5 0.7 all-gather.3.cloned.1.call-update
  7.3 2.5 copy.32
  9.8 2.2 copy.33
  12.0 8.5 %all-to-all-start = ((bf16[128,3,8,2,80]{0,4,3,1,2:T(8,128)(2,1)}), bf16[128,3,8,2,80]{0,4,3,1,2:T(8,128)(2,1)}, u32[]{:S(2)}, u32[]{:S(2)}) async-start(bf16[128,3,8,2,80]{0,4,3,1,2:T(8,128)(2,1)} %copy.33), calls=%async_computation | async-start | bytes 1966080 | tf_op jit(solution)/shard_map/all_to_all | solution.py:58
  20.4 0.0 all-gather.5.cloned.1.call-start
  20.5 37.9 %all-to-all-done = bf16[128,3,8,2,80]{0,4,3,1,2:T(8,128)(2,1)} async-done(((bf16[128,3,8,2,80]{0,4,3,1,2:T(8,128)(2,1)}), bf16[128,3,8,2,80]{0,4,3,1,2:T(8,128)(2,1)}, u32[]{:S(2)}, u32[]{:S(2)}) %all-to-all-start) | async-done | bytes 983072 | tf_op jit(solution)/shard_map/all_to_all | solution.py:58
  58.4 1.3 copy_bitcast_fusion
  59.7 1.0 slice_bitcast_fusion
  60.7 22.1 %while.10 = (s32[]{:T(128)}, bf16[2,512,2,80]{1,3,2,0:T(8,128)(2,1)}, s32[2]{0:T(128)S(1)}, bf16[1024,2,80]{0,2,1:T(8,128)(2,1)}, bf16[1024,2,80]{0,2,1:T(8,128)...) while((s32[]{:T(128)}, bf16[2,512,2,80]{1,3,2,0:T(8,128)(2,1)}, ...), condition=%wide.region_3.4_spmd, body=%wide.region_0.3_spmd.sunk | while | flops 340870144 | bytes 9380495 | solution.py:31
  60.7 0.7 dynamic_slice.22
  63.5 4.6 %fusion.154 = (f32[2,512]{1,0:T(2,128)S(1)}, f32[2,512,1024]{2,1,0:T(8,128)}) fusion(bf16[1024,2,80]{0,2,1:T(8,128)(2,1)} %get-tuple-element.120, bf16[1024,2,80]{0,2,1:T(8,128)(2,1)} %get-tuple-element.119, s32[]{:T(128)S(6)} %select_n.70), kind=kOutput, calls=%fused_computation.154.clone.1 | convolution fusion | flops 170918912 | bytes 4689924 | tf_op jit(solution)/shard_map/while/body/eval_jaxpr/sub | solution.py:25
  68.0 3.8 %fusion.155 = bf16[2,512,2,80]{1,3,2,0:T(8,128)(2,1)} fusion(bf16[2,512,2,80]{1,3,2,0:T(8,128)(2,1)} %get-tuple-element.108, s32[]{:T(128)} %get-tuple-element.107, bf16[1024,2,80]{0,2,1:T(8,128)(2,1)} %get-tuple-element.121, f32[2,512,1024]{2,1,0:T(8,128)} %get-tuple-element.96, f32[2,512]{1,0:T(2,128)S(1)} %get-tuple-element.97), kind=kOutput, calls=%fused_computation.11.clone.1 | convolution fusion | flops 169951232 | bytes 4690432 | tf_op jit(solution)/shard_map/while/body/eval_jaxpr/hqk,khd->qhd/dot_general | solution.py:27
  71.8 0.7 dynamic_slice.22
  74.6 4.5 %fusion.154 = (f32[2,512]{1,0:T(2,128)S(1)}, f32[2,512,1024]{2,1,0:T(8,128)}) fusion(bf16[1024,2,80]{0,2,1:T(8,128)(2,1)} %get-tuple-element.120, bf16[1024,2,80]{0,2,1:T(8,128)(2,1)} %get-tuple-element.119, s32[]{:T(128)S(6)} %select_n.70), kind=kOutput, calls=%fused_computation.154.clone.1 | convolution fusion | flops 170918912 | bytes 4689924 | tf_op jit(solution)/shard_map/while/body/eval_jaxpr/sub | solution.py:25
  79.1 3.7 %fusion.155 = bf16[2,512,2,80]{1,3,2,0:T(8,128)(2,1)} fusion(bf16[2,512,2,80]{1,3,2,0:T(8,128)(2,1)} %get-tuple-element.108, s32[]{:T(128)} %get-tuple-element.107, bf16[1024,2,80]{0,2,1:T(8,128)(2,1)} %get-tuple-element.121, f32[2,512,1024]{2,1,0:T(8,128)} %get-tuple-element.96, f32[2,512]{1,0:T(2,128)S(1)} %get-tuple-element.97), kind=kOutput, calls=%fused_computation.11.clone.1 | convolution fusion | flops 169951232 | bytes 4690432 | tf_op jit(solution)/shard_map/while/body/eval_jaxpr/hqk,khd->qhd/dot_general | solution.py:27
  82.8 0.0 copy-start.3
  82.8 0.0 copy-start.4
  82.8 2.0 copy.35
  84.9 1.9 reshape_reshape.3
  86.8 0.0 copy-start.2
  86.8 1.0 copy.36
  87.8 16.6 %all_to_all.43 = bf16[8,128,1,160]{1,3,2,0:T(8,128)(2,1)} all-to-all(bf16[8,128,1,160]{1,3,2,0:T(8,128)(2,1)S(1)} %copy.36), channel_id=1, replica_groups=mesh['seq'=8,'exp'=8,'img'=4] {'seq'}, dimensions={0} | all-to-all | bytes 655360 | tf_op jit(solution)/shard_map/all_to_all | solution.py:60
  104.4 0.0 all-gather.3.cloned.1.call-done
  104.4 2.8 fusion.139
  107.2 0.0 copy-start.1
  107.2 0.2 multiply_reduce_fusion.1
  107.4 0.6 copy-done.1
  108.1 0.0 copy-done.3
  108.1 0.0 copy-done.4
  108.1 0.9 add_convert_fusion.1
  109.0 0.0 all-gather.5.cloned.1.call-update
  109.0 0.0 copy-done.2
  109.0 0.1 copy.37
  109.1 2.5 select_reduce_fusion
  111.7 35.8 %all-gather.5.cloned.1.call-done = bf16[1024,1280]{1,0:T(8,128)(2,1)} async-done(((bf16[128,1280]{1,0:T(8,128)(2,1)}), bf16[1024,1280]{1,0:T(8,128)(2,1)}) %all-gather.5.cloned.1.call-update) | async-done | bytes 2621456 | tf_op jit(solution)/shard_map/all_gather | solution.py:79
  147.5 8.6 %scatter_custom_fusion = bf16[1536,1280]{1,0:T(8,128)(2,1)} fusion(s32[1024]{0:T(1024)S(1)} %bitcast.147, bf16[1024,1280]{1,0:T(8,128)(2,1)} %all-gather.5.cloned.1.call-done, bf16[]{:T(256)} %constant.31.clone.1), kind=kCustom, calls=%fused_computation.83 | custom fusion | bytes 3932672 | tf_op jit(solution)/shard_map/scatter | solution.py:80
  156.1 50.5 %all_to_all.44 = bf16[8,2,96,1280]{3,2,1,0:T(8,128)(2,1)} all-to-all(bf16[8,2,96,1280]{3,2,1,0:T(8,128)(2,1)} %bitcast.142), channel_id=1, replica_groups=mesh['seq'=8,'exp'=8,'img'=4] {'exp'}, dimensions={0} | all-to-all | bytes 7864320 | tf_op jit(solution)/shard_map/all_to_all | solution.py:82
  206.6 0.0 copy-done
  206.6 17.1 %fusion.43 = bf16[8,2,96,1280]{3,2,0,1:T(8,128)(2,1)} fusion(bf16[2,640,1280]{2,1,0:T(8,128)(2,1)S(1)} %copy-done, bf16[8,2,96,1280]{3,2,1,0:T(8,128)(2,1)} %all_to_all.44, bf16[2,1280,640]{2,1,0:T(8,128)(2,1)} %param.16), kind=kOutput, calls=%fused_computation.46 | convolution fusion | flops 5099028480 | bytes 14417920 | tf_op jit(solution)/shard_map/secf,efd->secd/dot_general | solution.py:87
  223.7 4.3 %copy.41 = bf16[8,2,96,1280]{3,2,1,0:T(8,128)(2,1)} copy(bf16[8,2,96,1280]{3,2,0,1:T(8,128)(2,1)} %fusion.43) | data formatting | bytes 7864320 | tf_op jit(solution)/shard_map/convert_element_type | solution.py:89
  228.0 4.5 %all-to-all-start.3 = ((bf16[8,2,96,1280]{3,2,1,0:T(8,128)(2,1)}), bf16[8,2,96,1280]{3,2,1,0:T(8,128)(2,1)}, u32[]{:S(2)}, u32[]{:S(2)}) async-start(bf16[8,2,96,1280]{3,2,1,0:T(8,128)(2,1)} %copy.41), calls=%async_computation.3 | async-start | bytes 7864320 | tf_op jit(solution)/shard_map/all_to_all | solution.py:90
  232.5 0.0 reduce-scatter.2.cloned.1.call-start
  232.6 50.5 %all-to-all-done.3 = bf16[8,2,96,1280]{3,2,1,0:T(8,128)(2,1)} async-done(((bf16[8,2,96,1280]{3,2,1,0:T(8,128)(2,1)}), bf16[8,2,96,1280]{3,2,1,0:T(8,128)(2,1)}, u32[]{:S(2)}, u32[]{:S(2)}) %all-to-all-start.3) | async-done | bytes 3932192 | tf_op jit(solution)/shard_map/all_to_all | solution.py:90
  283.1 9.2 %gather_fusion = bf16[1024,1280]{1,0:T(8,128)(2,1)} fusion(bf16[1536,1280]{1,0:T(8,128)(2,1)} %bitcast.27, s32[1024]{0:T(1024)S(1)} %broadcast_clamp_fusion), kind=kCustom, calls=%fused_computation | custom fusion | bytes 5246976 | tf_op jit(solution)/shard_map/jit(_take)/gather | solution.py:93
  292.3 3.5 %broadcast_select_fusion = bf16[1024,1280]{1,0:T(8,128)(2,1)} fusion(bf16[1024,1280]{1,0:T(8,128)(2,1)} %gather_fusion, pred[1024]{0:T(1024)(128)(4,1)S(1)} %compare_and_fusion), kind=kLoop, calls=%fused_computation.49 | loop fusion | flops 1310720 | bytes 5243904 | tf_op jit(solution)/shard_map/jit(_take)/select_n | solution.py:93
  295.9 0.0 reduce-scatter.2.cloned.1.call-update
  295.9 39.4 %reduce-scatter.2.cloned.1.call-done = bf16[128,1280]{1,0:T(8,128)(2,1)} async-done(((bf16[1024,1280]{1,0:T(8,128)(2,1)}), bf16[128,1280]{1,0:T(8,128)(2,1)}) %reduce-scatter.2.cloned.1.call-update) | async-done | bytes 327696 | tf_op jit(solution)/shard_map/reduce_scatter | solution.py:94
  335.3 1.9 fusion.93
  (9 shorter events, 0.1 us)
Async XLA Ops:
  6.5 200.1 %copy-start = (bf16[2,640,1280]{2,1,0:T(8,128)(2,1)S(1)}, bf16[2,640,1280]{2,1,0:T(8,128)(2,1)}, u32[]{:S(2)}) copy-start(bf16[2,640,1280]{2,1,0:T(8,128)(2,1)} %param.17) | copy-start | bytes 9830404
  6.5 97.9 %all-gather.3.cloned.1.call-start = ((), (), s32[]{:S(2)}) async-start(), calls=%async_computation.5 | async-start | bytes 3686400 | tf_op jit(solution)/shard_map/all_gather | solution.py:65
  12.0 46.4 %all-to-all-start = ((bf16[128,3,8,2,80]{0,4,3,1,2:T(8,128)(2,1)}), bf16[128,3,8,2,80]{0,4,3,1,2:T(8,128)(2,1)}, u32[]{:S(2)}, u32[]{:S(2)}) async-start(bf16[128,3,8,2,80]{0,4,3,1,2:T(8,128)(2,1)} %copy.33), calls=%async_computation | async-start | bytes 1966080 | tf_op jit(solution)/shard_map/all_to_all | solution.py:58
  20.4 127.1 %all-gather.5.cloned.1.call-start = ((), (), s32[]{:S(2)}) async-start(), calls=%async_computation.6 | async-start | bytes 2949120 | tf_op jit(solution)/shard_map/all_gather | solution.py:79
  82.8 25.2 %copy-start.3 = (f32[1280]{0:T(1024)S(1)}, f32[1280]{0:T(1024)}, u32[]{:S(2)}) copy-start(f32[1280]{0:T(1024)} %param.14) | copy-start | bytes 15364
  82.8 25.3 %copy-start.4 = (f32[1280]{0:T(1024)S(1)}, f32[1280]{0:T(1024)}, u32[]{:S(2)}) copy-start(f32[1280]{0:T(1024)} %param.13) | copy-start | bytes 15364
  86.8 22.2 %copy-start.2 = (s32[1,1024,1]{1,2,0:T(1,128)S(1)}, s32[1,1024,1]{1,2,0:T(1,128)}, u32[]{:S(2)}) copy-start(s32[1,1024,1]{1,2,0:T(1,128)} %param.15) | copy-start | bytes 12292
  107.2 0.9 copy-start.1
  228.0 55.1 %all-to-all-start.3 = ((bf16[8,2,96,1280]{3,2,1,0:T(8,128)(2,1)}), bf16[8,2,96,1280]{3,2,1,0:T(8,128)(2,1)}, u32[]{:S(2)}, u32[]{:S(2)}) async-start(bf16[8,2,96,1280]{3,2,1,0:T(8,128)(2,1)} %copy.41), calls=%async_computation.3 | async-start | bytes 7864320 | tf_op jit(solution)/shard_map/all_to_all | solution.py:90
  232.5 102.8 %reduce-scatter.2.cloned.1.call-start = ((), (), s32[]{:S(2)}) async-start(), calls=%async_computation.7 | async-start | bytes 2949120 | tf_op jit(solution)/shard_map/reduce_scatter | solution.py:94
Sparse Core Ops, SparseCore 0:
  9.1 67.2 all-gather.2
  109.1 38.3 all-gather.4
  296.0 39.2 reduce-scatter.1
where the time goes:
time: 344 us
  waiting for transfers between devices  164 us (48%)
  blocking collectives  67.1 us (20%)
  matrix products  36.5 us (11%)
  local copies, waits for them, and re-layouts  36.3 us (11%)
  between operations  13.2 us (4%)
  starting transfers between devices  13.1 us (4%)
  other arithmetic  9.21 us (3%)
  loops' own time  4.15 us (1%)
    all_to_all x1, blocking collectives, per_device(): lax.all_to_all(buffer, 'exp', split_axis=0, concat_axis=0, tiled=True)  50.5 us
    all_to_all x1, waiting for transfers between devices, per_device(): lax.all_to_all(pieces, 'exp', split_axis=0, concat_axis=0, tiled=True)  50.5 us
    reduce_scatter x1, waiting for transfers between devices, per_device(): lax.psum_scatter(per_token.astype(jnp.bfloat16), 'seq', scatter_dimension...  39.4 us
    all_to_all x1, waiting for transfers between devices, per_device(): lax.all_to_all(regrouped, 'seq', split_axis=2, concat_axis=0, tiled=True)  37.9 us
    all_gather x1, waiting for transfers between devices, per_device(): normed_all = lax.all_gather(normed, 'seq', axis=0, tiled=True)  35.8 us
    dot_general x1, matrix products, per_device(): jnp.einsum('secf,efd->secd', hidden, expert_down, preferred_element_type=...  17.1 us
    all_to_all x1, blocking collectives, per_device(): lax.all_to_all(attended, 'seq', split_axis=0, concat_axis=2, tiled=True)  16.6 us
    gather x1, local copies, waits for them, and re-layouts, per_device(): per_token = jnp.take(returned, slot_all, axis=0).astype(jnp.float32)  9.22 us
  transfers between devices with their start and end apart: 5, of which 4 were waited for; matrix products, arithmetic and copies ran while one was open for 10% of the time, Pallas kernels for 0%

commit v1 on v0

--- a/solution.py
+++ b/solution.py
@@ -76,7 +76,9 @@
     order_in_block = jnp.sum(before * blocks, axis=2).reshape(length)
     block_id = jnp.arange(length, dtype=jnp.int32) // tok_rows
     slot_all = ids_flat * capacity + block_id * cap_dev + order_in_block
-    normed_all = lax.all_gather(normed, "seq", axis=0, tiled=True)
+    normed_all = jnp.concatenate(
+        lax.all_to_all(jnp.stack([normed] * lax.axis_size("seq")), "seq", 0, 0), axis=0
+    )
     buffer = jnp.zeros((experts * capacity, model_width), jnp.bfloat16).at[slot_all].set(normed_all)
     buffer = buffer.reshape(exp_count, local_experts, capacity, model_width)
     arrived = lax.all_to_all(buffer, "exp", split_axis=0, concat_axis=0, tiled=True)

time: 344 us -> 379 us (1.10)
  waiting for transfers between devices: 164 us -> 190 us
  starting transfers between devices: 13.1 us -> 17.4 us
    all_to_all x0 -> x1, waiting for transfers between devices: none -> 59.3 us  [per_device(): lax.all_to_all(jnp.stack([normed] * lax.axis_size('seq')), 'seq', 0, 0)]
    all_gather x1 -> x0, waiting for transfers between devices: 35.8 us -> none  [per_device(): normed_all = lax.all_gather(normed, 'seq', axis=0, tiled=True)]
    all_to_all x0 -> x1, starting transfers between devices: none -> 4.39 us  [per_device(): lax.all_to_all(jnp.stack([normed] * lax.axis_size('seq')), 'seq', 0, 0)]
    all_to_all x1, waiting for transfers between devices: 50.5 us -> 54.5 us  [per_device(): lax.all_to_all(pieces, 'exp', split_axis=0, concat_axis=0, tiled=True)]
  transfers between devices with their start and end apart: 5 -> 5, of which waited for: 4 -> 4; matrix products, arithmetic and copies ran while one was open for 10% -> 9% of each run, Pallas kernels for 0% -> 0%
where the time goes in v1:
time: 379 us
  waiting for transfers between devices  190 us (50%)
  blocking collectives  70.8 us (19%)
  local copies, waits for them, and re-layouts  37.9 us (10%)
  matrix products  36.5 us (10%)
  starting transfers between devices  17.4 us (5%)
  between operations  13.5 us (4%)
  other arithmetic  8.49 us (2%)
  loops' own time  4.15 us (1%)
    all_to_all x1, waiting for transfers between devices, per_device(): lax.all_to_all(jnp.stack([normed] * lax.axis_size('seq')), 'seq', 0, 0)  59.3 us
    all_to_all x1, waiting for transfers between devices, per_device(): lax.all_to_all(pieces, 'exp', split_axis=0, concat_axis=0, tiled=True)  54.5 us
    all_to_all x1, blocking collectives, per_device(): lax.all_to_all(buffer, 'exp', split_axis=0, concat_axis=0, tiled=True)  54.2 us
    all_to_all x1, waiting for transfers between devices, per_device(): lax.all_to_all(regrouped, 'seq', split_axis=2, concat_axis=0, tiled=True)  37.9 us
    reduce_scatter x1, waiting for transfers between devices, per_device(): lax.psum_scatter(per_token.astype(jnp.bfloat16), 'seq', scatter_dimension...  37.4 us
    dot_general x1, matrix products, per_device(): jnp.einsum('secf,efd->secd', hidden, expert_down, preferred_element_type=...  17.1 us
    all_to_all x1, blocking collectives, per_device(): lax.all_to_all(attended, 'seq', split_axis=0, concat_axis=2, tiled=True)  16.6 us
    gather x1, local copies, waits for them, and re-layouts, per_device(): per_token = jnp.take(returned, slot_all, axis=0).astype(jnp.float32)  9.22 us
  transfers between devices with their start and end apart: 5, of which 4 were waited for; matrix products, arithmetic and copies ran while one was open for 9% of the time, Pallas kernels for 0%

profile of v1, /device:TPU:8, one launch (start us, length us, event | category | flops | bytes accessed | tf_op | source)
XLA Modules:
  0.0 378.6 jit_solution(4055620462331409286)
XLA Ops:
  6.5 0.0 copy-start
  6.5 0.0 all-gather.2.cloned.1.call-start
  6.5 0.7 all-gather.2.cloned.1.call-update
  7.3 2.5 copy.32
  9.8 2.2 copy.33
  12.0 8.5 %all-to-all-start = ((bf16[128,3,8,2,80]{0,4,3,1,2:T(8,128)(2,1)}), bf16[128,3,8,2,80]{0,4,3,1,2:T(8,128)(2,1)}, u32[]{:S(2)}, u32[]{:S(2)}) async-start(bf16[128,3,8,2,80]{0,4,3,1,2:T(8,128)(2,1)} %copy.33), calls=%async_computation | async-start | bytes 1966080 | tf_op jit(solution)/shard_map/all_to_all | solution.py:58
  20.4 37.9 %all-to-all-done = bf16[128,3,8,2,80]{0,4,3,1,2:T(8,128)(2,1)} async-done(((bf16[128,3,8,2,80]{0,4,3,1,2:T(8,128)(2,1)}), bf16[128,3,8,2,80]{0,4,3,1,2:T(8,128)(2,1)}, u32[]{:S(2)}, u32[]{:S(2)}) %all-to-all-start) | async-done | bytes 983072 | tf_op jit(solution)/shard_map/all_to_all | solution.py:58
  58.4 1.3 copy_bitcast_fusion
  59.7 1.0 slice_bitcast_fusion
  60.7 22.1 %while.10 = (s32[]{:T(128)}, bf16[2,512,2,80]{1,3,2,0:T(8,128)(2,1)}, s32[2]{0:T(128)S(1)}, bf16[1024,2,80]{0,2,1:T(8,128)(2,1)}, bf16[1024,2,80]{0,2,1:T(8,128)...) while((s32[]{:T(128)}, bf16[2,512,2,80]{1,3,2,0:T(8,128)(2,1)}, ...), condition=%wide.region_3.4_spmd, body=%wide.region_0.3_spmd.sunk | while | flops 340870144 | bytes 9380495 | solution.py:31
  60.7 0.7 dynamic_slice.22
  63.5 4.6 %fusion.154 = (f32[2,512]{1,0:T(2,128)S(1)}, f32[2,512,1024]{2,1,0:T(8,128)}) fusion(bf16[1024,2,80]{0,2,1:T(8,128)(2,1)} %get-tuple-element.120, bf16[1024,2,80]{0,2,1:T(8,128)(2,1)} %get-tuple-element.119, s32[]{:T(128)S(6)} %select_n.70), kind=kOutput, calls=%fused_computation.154.clone.1 | convolution fusion | flops 170918912 | bytes 4689924 | tf_op jit(solution)/shard_map/while/body/eval_jaxpr/sub | solution.py:25
  68.0 3.8 fusion.155
  71.8 0.7 dynamic_slice.22
  74.6 4.5 %fusion.154 = (f32[2,512]{1,0:T(2,128)S(1)}, f32[2,512,1024]{2,1,0:T(8,128)}) fusion(bf16[1024,2,80]{0,2,1:T(8,128)(2,1)} %get-tuple-element.120, bf16[1024,2,80]{0,2,1:T(8,128)(2,1)} %get-tuple-element.119, s32[]{:T(128)S(6)} %select_n.70), kind=kOutput, calls=%fused_computation.154.clone.1 | convolution fusion | flops 170918912 | bytes 4689924 | tf_op jit(solution)/shard_map/while/body/eval_jaxpr/sub | solution.py:25
  79.1 3.7 fusion.155
  82.8 0.0 copy-start.3
  82.8 0.0 copy-start.4
  82.8 2.0 copy.35
  84.9 1.9 reshape_reshape.3
  86.8 1.0 copy.36
  87.8 16.6 %all_to_all.48 = bf16[8,128,1,160]{1,3,2,0:T(8,128)(2,1)} all-to-all(bf16[8,128,1,160]{1,3,2,0:T(8,128)(2,1)S(1)} %copy.36), channel_id=1, replica_groups=mesh['seq'=8,'exp'=8,'img'=4] {'seq'}, dimensions={0} | all-to-all | bytes 655360 | tf_op jit(solution)/shard_map/all_to_all | solution.py:60
  104.4 0.0 all-gather.2.cloned.1.call-done
  104.4 2.8 fusion.139
  107.2 0.0 copy-start.1
  107.2 0.2 multiply_reduce_fusion.1
  107.4 0.6 copy-done.1
  108.1 0.0 copy-done.3
  108.1 0.0 copy-done.4
  108.1 0.2 add_convert_fusion.1
  108.2 0.0 copy-start.2
  108.3 1.7 stack.2
  109.9 4.4 %all-to-all-start.2 = ((bf16[8,128,1280]{2,1,0:T(8,128)(2,1)}), bf16[8,128,1280]{2,1,0:T(8,128)(2,1)}, u32[]{:S(2)}, u32[]{:S(2)}) async-start(bf16[8,128,1280]{2,1,0:T(8,128)(2,1)} %stack.2), calls=%async_computation.2 | async-start | bytes 5242880 | tf_op jit(solution)/shard_map/all_to_all | solution.py:80
  114.3 0.0 copy-done.2
  114.3 0.1 copy.37
  114.4 2.5 select_reduce_fusion
  117.1 59.3 %all-to-all-done.2 = bf16[8,128,1280]{2,1,0:T(8,128)(2,1)} async-done(((bf16[8,128,1280]{2,1,0:T(8,128)(2,1)}), bf16[8,128,1280]{2,1,0:T(8,128)(2,1)}, u32[]{:S(2)}, u32[]{:S(2)}) %all-to-all-start.2) | async-done | bytes 2621472 | tf_op jit(solution)/shard_map/all_to_all | solution.py:80
  176.3 8.6 %scatter_custom_fusion = bf16[1536,1280]{1,0:T(8,128)(2,1)} fusion(s32[1024]{0:T(1024)S(1)} %bitcast.148, bf16[1024,1280]{1,0:T(8,128)(2,1)} %bitcast.19, bf16[]{:T(256)} %constant.31.clone.1), kind=kCustom, calls=%fused_computation.83 | custom fusion | bytes 3932672 | tf_op jit(solution)/shard_map/scatter | solution.py:82
  184.9 54.2 %all_to_all.49 = bf16[8,2,96,1280]{3,2,1,0:T(8,128)(2,1)} all-to-all(bf16[8,2,96,1280]{3,2,1,0:T(8,128)(2,1)} %bitcast.143), channel_id=1, replica_groups=mesh['seq'=8,'exp'=8,'img'=4] {'exp'}, dimensions={0} | all-to-all | bytes 7864320 | tf_op jit(solution)/shard_map/all_to_all | solution.py:84
  239.1 0.0 copy-done
  239.1 17.1 %fusion.43 = bf16[8,2,96,1280]{3,2,0,1:T(8,128)(2,1)} fusion(bf16[2,640,1280]{2,1,0:T(8,128)(2,1)S(1)} %copy-done, bf16[8,2,96,1280]{3,2,1,0:T(8,128)(2,1)} %all_to_all.49, bf16[2,1280,640]{2,1,0:T(8,128)(2,1)} %param.16), kind=kOutput, calls=%fused_computation.46 | convolution fusion | flops 5099028480 | bytes 14417920 | tf_op jit(solution)/shard_map/secf,efd->secd/dot_general | solution.py:89
  256.2 4.3 %copy.41 = bf16[8,2,96,1280]{3,2,1,0:T(8,128)(2,1)} copy(bf16[8,2,96,1280]{3,2,0,1:T(8,128)(2,1)} %fusion.43) | data formatting | bytes 7864320 | tf_op jit(solution)/shard_map/convert_element_type | solution.py:91
  260.5 4.5 %all-to-all-start.4 = ((bf16[8,2,96,1280]{3,2,1,0:T(8,128)(2,1)}), bf16[8,2,96,1280]{3,2,1,0:T(8,128)(2,1)}, u32[]{:S(2)}, u32[]{:S(2)}) async-start(bf16[8,2,96,1280]{3,2,1,0:T(8,128)(2,1)} %copy.41), calls=%async_computation.4 | async-start | bytes 7864320 | tf_op jit(solution)/shard_map/all_to_all | solution.py:92
  265.0 0.0 reduce-scatter.2.cloned.1.call-start
  265.1 54.5 %all-to-all-done.4 = bf16[8,2,96,1280]{3,2,1,0:T(8,128)(2,1)} async-done(((bf16[8,2,96,1280]{3,2,1,0:T(8,128)(2,1)}), bf16[8,2,96,1280]{3,2,1,0:T(8,128)(2,1)}, u32[]{:S(2)}, u32[]{:S(2)}) %all-to-all-start.4) | async-done | bytes 3932192 | tf_op jit(solution)/shard_map/all_to_all | solution.py:92
  319.7 9.2 %gather_fusion = bf16[1024,1280]{1,0:T(8,128)(2,1)} fusion(bf16[1536,1280]{1,0:T(8,128)(2,1)} %bitcast.28, s32[1024]{0:T(1024)S(1)} %broadcast_clamp_fusion), kind=kCustom, calls=%fused_computation | custom fusion | bytes 5246976 | tf_op jit(solution)/shard_map/jit(_take)/gather | solution.py:95
  328.9 3.5 broadcast_select_fusion
  332.4 0.0 reduce-scatter.2.cloned.1.call-update
  332.5 37.4 %reduce-scatter.2.cloned.1.call-done = bf16[128,1280]{1,0:T(8,128)(2,1)} async-done(((bf16[1024,1280]{1,0:T(8,128)(2,1)}), bf16[128,1280]{1,0:T(8,128)(2,1)}) %reduce-scatter.2.cloned.1.call-update) | async-done | bytes 327696 | tf_op jit(solution)/shard_map/reduce_scatter | solution.py:96
  369.8 1.9 fusion.93
  (9 shorter events, 0.1 us)
Async XLA Ops:
  6.5 232.6 %copy-start = (bf16[2,640,1280]{2,1,0:T(8,128)(2,1)S(1)}, bf16[2,640,1280]{2,1,0:T(8,128)(2,1)}, u32[]{:S(2)}) copy-start(bf16[2,640,1280]{2,1,0:T(8,128)(2,1)} %param.17) | copy-start | bytes 9830404
  6.5 97.8 %all-gather.2.cloned.1.call-start = ((), (), s32[]{:S(2)}) async-start(), calls=%async_computation.6 | async-start | bytes 3686400 | tf_op jit(solution)/shard_map/all_gather | solution.py:65
  12.0 46.4 %all-to-all-start = ((bf16[128,3,8,2,80]{0,4,3,1,2:T(8,128)(2,1)}), bf16[128,3,8,2,80]{0,4,3,1,2:T(8,128)(2,1)}, u32[]{:S(2)}, u32[]{:S(2)}) async-start(bf16[128,3,8,2,80]{0,4,3,1,2:T(8,128)(2,1)} %copy.33), calls=%async_computation | async-start | bytes 1966080 | tf_op jit(solution)/shard_map/all_to_all | solution.py:58
  82.8 25.2 %copy-start.3 = (f32[1280]{0:T(1024)S(1)}, f32[1280]{0:T(1024)}, u32[]{:S(2)}) copy-start(f32[1280]{0:T(1024)} %param.14) | copy-start | bytes 15364
  82.8 25.2 %copy-start.4 = (f32[1280]{0:T(1024)S(1)}, f32[1280]{0:T(1024)}, u32[]{:S(2)}) copy-start(f32[1280]{0:T(1024)} %param.13) | copy-start | bytes 15364
  107.2 0.9 copy-start.1
  108.2 6.1 %copy-start.2 = (s32[1,1024,1]{1,2,0:T(1,128)S(1)}, s32[1,1024,1]{1,2,0:T(1,128)}, u32[]{:S(2)}) copy-start(s32[1,1024,1]{1,2,0:T(1,128)} %param.15) | copy-start | bytes 12292
  109.9 66.4 %all-to-all-start.2 = ((bf16[8,128,1280]{2,1,0:T(8,128)(2,1)}), bf16[8,128,1280]{2,1,0:T(8,128)(2,1)}, u32[]{:S(2)}, u32[]{:S(2)}) async-start(bf16[8,128,1280]{2,1,0:T(8,128)(2,1)} %stack.2), calls=%async_computation.2 | async-start | bytes 5242880 | tf_op jit(solution)/shard_map/all_to_all | solution.py:80
  260.5 59.2 %all-to-all-start.4 = ((bf16[8,2,96,1280]{3,2,1,0:T(8,128)(2,1)}), bf16[8,2,96,1280]{3,2,1,0:T(8,128)(2,1)}, u32[]{:S(2)}, u32[]{:S(2)}) async-start(bf16[8,2,96,1280]{3,2,1,0:T(8,128)(2,1)} %copy.41), calls=%async_computation.4 | async-start | bytes 7864320 | tf_op jit(solution)/shard_map/all_to_all | solution.py:92
  265.0 104.8 %reduce-scatter.2.cloned.1.call-start = ((), (), s32[]{:S(2)}) async-start(), calls=%async_computation.7 | async-start | bytes 2949120 | tf_op jit(solution)/shard_map/reduce_scatter | solution.py:96
Sparse Core Ops, SparseCore 0:
  9.1 67.2 all-gather.1
  332.6 37.1 reduce-scatter.1
